TPU v7x, 32 devices: a whole 2x2x4 slice. The times are simulated.
32 devices in a mesh: groups: 1, rows: 32 (over z, y, x, core).
Axes of the slice: x: 2, y: 2, z: 4, core: 2. Of those that a mesh axis runs over, the one named last changes fastest.
Arguments:
- acts: bfloat16 [4096, 2, 4096], P(('groups', 'rows')), may hold values from -6 to 6
- grads_out: bfloat16 [4096, 2, 4096], P(('groups', 'rows')), may hold values from -6 to 6
- lengths: int32 [32], P('groups'), may hold values from 1 to 512, 4096 in all
- valid: int32 [4096], P(('groups', 'rows')), may hold values 0 or 1
- proj_in: bfloat16 [4096, 128], replicated, may hold values from -0.09375 to 0.09375
- proj_out: bfloat16 [4096, 128], replicated, may hold values from -0.09375 to 0.09375
- fisher_inv: float32 [2, 4096, 4096], P(None, 'rows'), may hold values from -1 to 2, as said below
- database: float32 [4096, 2, 4096], P(('groups', 'rows')), may hold values from -250 to 250
Outputs:
- zscores: float32 [32, 4096], P(None, ('groups', 'rows'))
Inputs may be any that keep to these rules, and one draw needn't show every extreme that they name: The lengths sum to 4096; the largest is exactly 512. `fisher_inv`: each of the 2 blocks is symmetric.
All inputs are finite; a program needn't handle non-finite values. No bound on the sum of `valid` on one device may be relied on, other than what follows from the above.
Results may differ from a plain program's by a relative error of at most 0.0042.
Values sent between devices are 32-bit elements; how exact they have to be, the bound alone decides.
No kernel may reach another device: no remote copies, remote signals or barrier semaphores. Data moves between devices by JAX's collectives and lax.ppermute only.
A program may use at most 64 MiB of HBM per device.

v0:
```python
import jax
import jax.numpy as jnp
from jax import lax
from jax.sharding import PartitionSpec as P


def shards(acts, grads_out, lengths, valid, proj_in, proj_out, fisher_inv, database):
    tok_rows = acts.shape[0]
    modules = acts.shape[1]
    proj_rank = proj_in.shape[1] // modules
    queries = lengths.shape[0]
    flat_width = proj_rank * proj_rank
    first_pos = lax.axis_index("rows") * tok_rows
    positions = first_pos + jnp.arange(tok_rows, dtype=jnp.int32)
    seg_ends = jnp.cumsum(lengths)
    segment = jnp.sum((seg_ends[None, :] <= positions[:, None]).astype(jnp.int32), axis=1)
    selector = (
        (segment[:, None] == jnp.arange(queries, dtype=jnp.int32)[None, :]) & (valid[:, None] == 1)
    ).astype(jnp.bfloat16)
    module_sums = []
    for m in range(modules):
        act_proj = jnp.dot(
            acts[:, m, :],
            proj_in[:, m * proj_rank : (m + 1) * proj_rank],
            preferred_element_type=jnp.float32,
        ).astype(jnp.bfloat16)
        grad_proj = jnp.dot(
            grads_out[:, m, :],
            proj_out[:, m * proj_rank : (m + 1) * proj_rank],
            preferred_element_type=jnp.float32,
        ).astype(jnp.bfloat16)
        spread = (selector[:, :, None] * grad_proj[:, None, :]).reshape(
            tok_rows, queries * proj_rank
        )
        module_sum = lax.dot_general(
            spread, act_proj, (((0,), (0,)), ((), ())), preferred_element_type=jnp.float32
        )
        module_sums.append(module_sum.reshape(queries, flat_width))
    partial_value = jnp.stack(module_sums, axis=1)
    summed = lax.psum(partial_value, "rows")
    precond_cols = jnp.einsum("qmk,mck->qmc", summed, fisher_inv, precision=lax.Precision.HIGHEST)
    scores = jnp.einsum(
        "qmk,nmk->qn",
        lax.all_gather(precond_cols, "rows", axis=2, tiled=True),
        database,
        precision=lax.Precision.HIGHEST,
    )
    db_count = database.shape[0] * lax.axis_size("rows")
    first_moment, second_moment = lax.psum(
        (jnp.sum(scores, axis=1), jnp.sum(scores * scores, axis=1)), "rows"
    )
    avg_score = first_moment / db_count
    variance = second_moment / db_count - avg_score * avg_score
    centred = scores - avg_score[:, None]
    return centred * lax.rsqrt(variance + 1e-06)[:, None]


def solution(mesh):
    placed = (
        P(("groups", "rows"), None, None),
        P(("groups", "rows"), None, None),
        P("groups"),
        P(("groups", "rows")),
        P(),
        P(),
        P(None, "rows", None),
        P(("groups", "rows"), None, None),
    )
    return jax.shard_map(
        shards, mesh=mesh, in_specs=placed, out_specs=P(None, ("groups", "rows")), check_vma=False
    )
```

profile of v0, /device:TPU:0, one launch (start us, length us, event | category | flops | bytes accessed | tf_op | source)
XLA Modules:
  0.0 286.0 jit_solution(3558763104719825832)
XLA Ops:
  6.5 0.0 all-reduce.3.cloned.1.call-start
  6.5 0.0 copy-start.4
  6.5 6.1 %fusion.17 = (bf16[128,1,4096]{2,1,0:T(2,128)(2,1)S(1)}, bf16[128,1,4096]{2,1,0:T(2,128)(2,1)S(1)}) fusion(bf16[128,2,4096]{2,1,0:T(2,128)(2,1)} %param.9), kind=kLoop, calls=%fused_computation.33 | loop fusion | bytes 4194304 | tf_op jit(solution)/shard_map/slice | solution.py:28
  12.7 0.0 copy-done.4
  12.7 0.0 copy-start.3
  12.7 0.0 copy-start.5
  12.7 0.0 copy-start
  12.7 1.6 convolution_convert_fusion.1
  14.4 1.3 convolution_convert_fusion.3
  15.7 0.0 copy-done.3
  15.7 0.1 copy.21
  15.8 0.1 reduce-window.8
  15.8 0.1 reduce
  16.0 0.0 copy-done.5
  16.0 0.0 copy-done
  16.0 0.0 copy-start.2
  16.0 5.8 %fusion.16 = (bf16[128,1,4096]{2,1,0:T(2,128)(2,1)}, bf16[128,1,4096]{2,1,0:T(2,128)(2,1)}) fusion(bf16[128,2,4096]{2,1,0:T(2,128)(2,1)S(1)} %copy-done), kind=kLoop, calls=%fused_computation.32 | loop fusion | bytes 4194304 | tf_op jit(solution)/shard_map/slice | solution.py:23
  21.9 0.1 convert_reduce_fusion
  22.0 1.1 broadcast_multiply_fusion.1
  23.0 0.0 copy-done.2
  23.0 0.0 copy-start.1
  23.0 4.6 %fusion.2 = f32[2048,64]{1,0:T(8,128)} fusion(bf16[128,2048]{0,1:T(8,128)(2,1)} %bitcast.27, bf16[128,1,4096]{2,1,0:T(2,128)(2,1)} %get-tuple-element.9, bf16[4096,128]{1,0:T(8,128)(2,1)S(1)} %copy-done.2), kind=kOutput, calls=%fused_computation.7 | convolution fusion | flops 100671488 | bytes 3145728 | tf_op jit(solution)/shard_map/dot_general | solution.py:35
  27.6 2.4 stack_reshape.6
  30.0 0.0 copy-done.1
  30.0 4.0 %fusion.3 = f32[2048,64]{1,0:T(8,128)} fusion(bf16[128,2048]{0,1:T(8,128)(2,1)} %bitcast.26, bf16[128,1,4096]{2,1,0:T(2,128)(2,1)S(1)} %copy-done.1, bf16[4096,128]{1,0:T(8,128)(2,1)S(1)} %copy-done.2), kind=kOutput, calls=%fused_computation.8 | convolution fusion | flops 100671488 | bytes 3145728 | tf_op jit(solution)/shard_map/dot_general | solution.py:35
  34.0 1.6 stack_reshape.7
  35.6 2.1 pad_maximum_fusion
  37.7 0.0 all-reduce.3.cloned.1.call-update
  37.8 0.2 all-gather.2.cloned.1.call-start
  38.0 133.4 %all-reduce.3.cloned.1.call-done = f32[32,2,4096]{2,0,1:T(8,128)} async-done(((f32[32,2,4096]{2,0,1:T(8,128)}), f32[32,2,4096]{2,0,1:T(8,128)}) %all-reduce.3.cloned.1.call-update) | async-done | bytes 1048592 | tf_op jit(solution)/shard_map/psum | solution.py:40
  171.4 7.3 %convolution_bitcast_fusion = f32[32,2,128]{2,0,1:T(8,128)} fusion(f32[32,2,4096]{2,0,1:T(8,128)} %all-reduce.3.cloned.1.call-done, f32[2,128,4096]{2,1,0:T(8,128)} %param.14), kind=kOutput, calls=%fused_computation.2 | convolution fusion | flops 402653184 | bytes 5275648 | tf_op jit(solution)/shard_map/qmk,mck->qmc/dot_general | solution.py:41
  178.7 0.0 all-gather.2.cloned.1.call-update
  178.8 51.4 %all-gather.2.cloned.1.call-done = f32[32,2,4096]{2,0,1:T(8,128)} async-done(((f32[32,2,128]{2,0,1:T(8,128)}), f32[32,2,4096]{2,0,1:T(8,128)}) %all-gather.2.cloned.1.call-update) | async-done | bytes 1048592 | tf_op jit(solution)/shard_map/all_gather | solution.py:44
  230.2 8.2 %fusion.15 = (f32[32]{0:T(128)S(1)}, f32[32]{0:T(128)S(1)}, f32[32,128]{1,0:T(8,128)S(1)}) fusion(f32[32,2,4096]{2,0,1:T(8,128)} %all-gather.2.cloned.1.call-done, f32[128,2,4096]{2,1,0:T(2,128)} %param.15), kind=kOutput, calls=%fused_computation.31 | convolution fusion | flops 402665408 | bytes 5259520 | tf_op jit(solution)/shard_map/qmk,nmk->qn/dot_general | solution.py:42
  238.3 40.1 %all-reduce = (f32[32]{0:T(128)S(1)}, f32[32]{0:T(128)S(1)}) all-reduce(f32[32]{0:T(128)S(1)} %get-tuple-element.6, f32[32]{0:T(128)S(1)} %get-tuple-element.5), channel_id=1, replica_groups=mesh['groups'=1,'rows'=32] {'rows'}, use_global_device_ids=true, to_apply=%region_6.7 | all-reduce | flops 64 | bytes 512 | tf_op jit(solution)/shard_map/psum | solution.py:49
  278.5 0.7 subtract_multiply_fusion
  (4 shorter events, 0.0 us)
Async XLA Ops:
  6.5 164.9 %all-reduce.3.cloned.1.call-start = ((), (), s32[]{:S(2)}) async-start(), calls=%async_computation | async-start | bytes 2097152 | tf_op jit(solution)/shard_map/psum | solution.py:40
  6.5 6.1 %copy-start.4 = (bf16[4096,128]{1,0:T(8,128)(2,1)S(1)}, bf16[4096,128]{1,0:T(8,128)(2,1)}, u32[]{:S(2)}) copy-start(bf16[4096,128]{1,0:T(8,128)(2,1)} %param.13) | copy-start | bytes 3145732
  12.7 3.0 %copy-start.3 = (s32[32]{0:T(128)S(1)}, s32[32]{0:T(128)}, u32[]{:S(2)}) copy-start(s32[32]{0:T(128)} %param.10) | copy-start | bytes 388
  12.7 3.3 %copy-start.5 = (s32[128]{0:T(128)S(1)}, s32[128]{0:T(128)}, u32[]{:S(2)}) copy-start(s32[128]{0:T(128)} %param.11) | copy-start | bytes 1540
  12.7 3.3 %copy-start = (bf16[128,2,4096]{2,1,0:T(2,128)(2,1)S(1)}, bf16[128,2,4096]{2,1,0:T(2,128)(2,1)}, u32[]{:S(2)}) copy-start(bf16[128,2,4096]{2,1,0:T(2,128)(2,1)} %param.8) | copy-start | bytes 6291460
  16.0 7.0 %copy-start.2 = (bf16[4096,128]{1,0:T(8,128)(2,1)S(1)}, bf16[4096,128]{1,0:T(8,128)(2,1)}, u32[]{:S(2)}) copy-start(bf16[4096,128]{1,0:T(8,128)(2,1)} %param.12) | copy-start | bytes 3145732
  23.0 7.0 %copy-start.1 = (bf16[128,1,4096]{2,1,0:T(2,128)(2,1)S(1)}, bf16[128,1,4096]{2,1,0:T(2,128)(2,1)}, u32[]{:S(2)}) copy-start(bf16[128,1,4096]{2,1,0:T(2,128)(2,1)} %get-tuple-element.10) | copy-start | bytes 3145732
  37.8 192.4 %all-gather.2.cloned.1.call-start = ((), (), s32[]{:S(2)}) async-start(), calls=%async_computation.1 | async-start | bytes 1081344 | tf_op jit(solution)/shard_map/all_gather | solution.py:44
Sparse Core Ops, SparseCore 0:
  37.9 133.4 all-reduce.2
  178.9 51.2 all-gather.1
where the time goes:
time: 286 us
  waiting for transfers between devices  185 us (65%)
  blocking collectives  40.1 us (14%)
  matrix products  27.1 us (9%)
  local copies, waits for them, and re-layouts  16 us (6%)
  between operations  13.5 us (5%)
  other arithmetic  4.19 us (1%)
    psum x1, waiting for transfers between devices, shards(): summed = lax.psum(partial_value, 'rows')  133 us
    all_gather x1, waiting for transfers between devices, shards(): lax.all_gather(precond_cols, 'rows', axis=2, tiled=True)  51.4 us
    psum x1, blocking collectives, shards(): lax.psum((jnp.sum(scores, axis=1), jnp.sum(scores * scores, axis=1)), 'ro...  40.1 us
    dot_general x2, matrix products, shards(): lax.dot_general(spread, act_proj, (((0,), (0,)), ((), ())), preferred_ele...  8.6 us
    dot_general x1, matrix products, shards(): jnp.einsum('qmk,nmk->qn', lax.all_gather(precond_cols, 'rows', axis=2, ti...  8.16 us
    dot_general x1, matrix products, shards(): jnp.einsum('qmk,mck->qmc', summed, fisher_inv, precision=lax.Precision.HI...  7.35 us
    slice x1, local copies, waits for them, and re-layouts, shards(): grads_out[:, m, :]  6.11 us
    slice x1, local copies, waits for them, and re-layouts, shards(): acts[:, m, :]  5.84 us
  transfers between devices with their start and end apart: 2, of which 2 were waited for; matrix products, arithmetic and copies ran while one was open for 0% of the time, Pallas kernels for 0%

commit v1 on v0

--- a/solution.py
+++ b/solution.py
@@ -37,7 +37,7 @@
         )
         module_sums.append(module_sum.reshape(queries, flat_width))
     partial_value = jnp.stack(module_sums, axis=1)
-    summed = lax.psum(partial_value, "rows")
+    summed = jnp.sum(lax.all_gather(partial_value, "rows"), axis=0)
     precond_cols = jnp.einsum("qmk,mck->qmc", summed, fisher_inv, precision=lax.Precision.HIGHEST)
     scores = jnp.einsum(
         "qmk,nmk->qn",

time: 286 us -> 362 us (1.27)
  waiting for transfers between devices: 185 us -> 248 us
  other arithmetic: 4.19 us -> 16.4 us
    all_gather x0 -> x1, waiting for transfers between devices: none -> 197 us  [shards(): summed = jnp.sum(lax.all_gather(partial_value, 'rows'), axis=0)]
    psum x1 -> x0, waiting for transfers between devices: 133 us -> none  [shards(): summed = lax.psum(partial_value, 'rows')]
    reduce_sum x0 -> x1, other arithmetic: none -> 11.7 us  [shards(): summed = jnp.sum(lax.all_gather(partial_value, 'rows'), axis=0)]
where the time goes in v1:
time: 362 us; the launch traced here: 361 us
  waiting for transfers between devices  248 us (69%)
  blocking collectives  40.1 us (11%)
  matrix products  26.1 us (7%)
  local copies, waits for them, and re-layouts  17.2 us (5%)
  other arithmetic  16.4 us (5%)
  between operations  13.5 us (4%)
    all_gather x1, waiting for transfers between devices, shards(): summed = jnp.sum(lax.all_gather(partial_value, 'rows'), axis=0)  197 us
    all_gather x1, waiting for transfers between devices, shards(): lax.all_gather(precond_cols, 'rows', axis=2, tiled=True)  50.6 us
    psum x1, blocking collectives, shards(): lax.psum((jnp.sum(scores, axis=1), jnp.sum(scores * scores, axis=1)), 'ro...  40.1 us
    reduce_sum x1, other arithmetic, shards(): summed = jnp.sum(lax.all_gather(partial_value, 'rows'), axis=0)  11.7 us
    dot_general x2, matrix products, shards(): lax.dot_general(spread, act_proj, (((0,), (0,)), ((), ())), preferred_ele...  8.48 us
    dot_general x1, matrix products, shards(): jnp.einsum('qmk,nmk->qn', lax.all_gather(precond_cols, 'rows', axis=2, ti...  8.16 us
    slice x1, local copies, waits for them, and re-layouts, shards(): acts[:, m, :]  7.65 us
  transfers between devices with their start and end apart: 2, of which 2 were waited for; matrix products, arithmetic and copies ran while one was open for 0% of the time, Pallas kernels for 0%

profile of v1, /device:TPU:0, one launch (start us, length us, event | category | flops | bytes accessed | tf_op | source)
XLA Modules:
  0.0 361.1 jit_solution(4628926813735376383)
XLA Ops:
  6.5 0.0 all-gather.6.cloned.1.call-start
  6.5 0.7 broadcast_compare_fusion
  7.2 0.7 copy.29
  7.9 0.1 reduce-window.8
  8.0 0.1 reduce
  8.1 0.0 copy-start
  8.1 7.6 %fusion.16 = (bf16[128,1,4096]{2,1,0:T(2,128)(2,1)}, bf16[128,1,4096]{2,1,0:T(2,128)(2,1)S(1)}) fusion(bf16[128,2,4096]{2,1,0:T(2,128)(2,1)} %param.8), kind=kLoop, calls=%fused_computation.32 | loop fusion | bytes 4194304 | tf_op jit(solution)/shard_map/slice | solution.py:23
  15.8 0.0 copy-done
  15.8 0.0 copy-start.2
  15.8 4.8 %fusion.17 = (bf16[128,1,4096]{2,1,0:T(2,128)(2,1)S(1)}, bf16[128,1,4096]{2,1,0:T(2,128)(2,1)S(1)}) fusion(bf16[128,2,4096]{2,1,0:T(2,128)(2,1)S(1)} %copy-done), kind=kLoop, calls=%fused_computation.33 | loop fusion | bytes 4194304 | tf_op jit(solution)/shard_map/slice | solution.py:28
  20.6 0.0 copy-done.2
  20.6 1.3 convolution_convert_fusion.3
  21.9 0.0 copy-start.1
  22.0 1.6 convolution_convert_fusion.1
  23.6 0.1 convert_reduce_fusion
  23.7 1.0 broadcast_multiply_fusion.1
  24.7 0.0 copy-done.1
  24.7 4.5 %fusion.2 = f32[2048,64]{1,0:T(8,128)} fusion(bf16[128,2048]{0,1:T(8,128)(2,1)} %bitcast.29, bf16[128,1,4096]{2,1,0:T(2,128)(2,1)} %get-tuple-element.9, bf16[4096,128]{1,0:T(8,128)(2,1)S(1)} %copy-done.1), kind=kOutput, calls=%fused_computation.7 | convolution fusion | flops 100671488 | bytes 3145728 | tf_op jit(solution)/shard_map/dot_general | solution.py:35
  29.2 2.4 stack_reshape.6
  31.6 4.0 %fusion.3 = f32[2048,64]{1,0:T(8,128)} fusion(bf16[128,2048]{0,1:T(8,128)(2,1)} %bitcast.28, bf16[128,1,4096]{2,1,0:T(2,128)(2,1)S(1)} %get-tuple-element.10, bf16[4096,128]{1,0:T(8,128)(2,1)S(1)} %copy-done.1), kind=kOutput, calls=%fused_computation.8 | convolution fusion | flops 100671488 | bytes 3145728 | tf_op jit(solution)/shard_map/dot_general | solution.py:35
  35.6 1.6 stack_reshape.7
  37.2 2.1 pad_maximum_fusion
  39.3 0.0 all-gather.6.cloned.1.call-update
  39.3 0.2 all-gather.4.cloned.1.call-start
  39.6 196.9 %all-gather.6.cloned.1.call-done = f32[1024,2,4096]{2,0,1:T(8,128)} async-done(((f32[32,2,4096]{2,0,1:T(8,128)}), f32[1024,2,4096]{2,0,1:T(8,128)}) %all-gather.6.cloned.1.call-update) | async-done | bytes 33554448 | tf_op jit(solution)/shard_map/all_gather | solution.py:40
  236.4 11.7 %reduce_sum.37 = f32[32,2,4096]{2,0,1:T(8,128)S(1)} reduce(f32[32,32,2,4096]{3,1,0,2:T(8,128)} %bitcast.27, f32[]{:T(128)} %constant.18.clone.1), dimensions={0}, to_apply=%region_2.3 | reduce | flops 8126464 | bytes 34603012 | tf_op jit(solution)/shard_map/reduce_sum | solution.py:40
  248.1 6.5 %convolution_bitcast_fusion = f32[32,2,128]{2,0,1:T(8,128)} fusion(f32[32,2,4096]{2,0,1:T(8,128)S(1)} %reduce_sum.37, f32[2,128,4096]{2,1,0:T(8,128)} %param.14), kind=kOutput, calls=%fused_computation.2 | convolution fusion | flops 402653184 | bytes 5275648 | tf_op jit(solution)/shard_map/qmk,mck->qmc/dot_general | solution.py:41
  254.6 0.0 all-gather.4.cloned.1.call-update
  254.6 50.6 %all-gather.4.cloned.1.call-done = f32[32,2,4096]{2,0,1:T(8,128)} async-done(((f32[32,2,128]{2,0,1:T(8,128)}), f32[32,2,4096]{2,0,1:T(8,128)}) %all-gather.4.cloned.1.call-update) | async-done | bytes 1048592 | tf_op jit(solution)/shard_map/all_gather | solution.py:44
  305.2 8.2 %fusion.15 = (f32[32]{0:T(128)S(1)}, f32[32]{0:T(128)S(1)}, f32[32,128]{1,0:T(8,128)S(1)}) fusion(f32[32,2,4096]{2,0,1:T(8,128)} %all-gather.4.cloned.1.call-done, f32[128,2,4096]{2,1,0:T(2,128)} %param.15), kind=kOutput, calls=%fused_computation.31 | convolution fusion | flops 402665408 | bytes 5259520 | tf_op jit(solution)/shard_map/qmk,nmk->qn/dot_general | solution.py:42
  313.4 40.1 %all-reduce = (f32[32]{0:T(128)S(1)}, f32[32]{0:T(128)S(1)}) all-reduce(f32[32]{0:T(128)S(1)} %get-tuple-element.6, f32[32]{0:T(128)S(1)} %get-tuple-element.5), channel_id=1, replica_groups=mesh['groups'=1,'rows'=32] {'rows'}, use_global_device_ids=true, to_apply=%region_6.7 | all-reduce | flops 64 | bytes 512 | tf_op jit(solution)/shard_map/psum | solution.py:49
  353.5 0.7 subtract_multiply_fusion
  (3 shorter events, 0.0 us)
Async XLA Ops:
  6.5 229.9 %all-gather.6.cloned.1.call-start = ((), (), s32[]{:S(2)}) async-start(), calls=%async_computation.1 | async-start | bytes 34603008 | tf_op jit(solution)/shard_map/all_gather | solution.py:40
  8.1 7.7 %copy-start = (bf16[128,2,4096]{2,1,0:T(2,128)(2,1)S(1)}, bf16[128,2,4096]{2,1,0:T(2,128)(2,1)}, u32[]{:S(2)}) copy-start(bf16[128,2,4096]{2,1,0:T(2,128)(2,1)} %param.9) | copy-start | bytes 6291460
  15.8 4.8 %copy-start.2 = (bf16[4096,128]{1,0:T(8,128)(2,1)S(1)}, bf16[4096,128]{1,0:T(8,128)(2,1)}, u32[]{:S(2)}) copy-start(bf16[4096,128]{1,0:T(8,128)(2,1)} %param.13) | copy-start | bytes 3145732
  21.9 2.8 copy-start.1
  39.3 265.9 %all-gather.4.cloned.1.call-start = ((), (), s32[]{:S(2)}) async-start(), calls=%async_computation | async-start | bytes 1081344 | tf_op jit(solution)/shard_map/all_gather | solution.py:44
Sparse Core Ops, SparseCore 0:
  39.4 196.9 all-gather.5
  254.7 50.4 all-gather.3
